TPU v7x, 1024 devices: a whole 8x8x8 slice. The times are simulated.
1024 devices in a mesh: section: 16 (over y, z_lo), dp: 64 (over x, z_hi, core).
Axes of the slice: x: 8, y: 8, z: 8 (z_hi: 4, z_lo: 2; z = z_hi * 2 + z_lo), core: 2. Of those that a mesh axis runs over, the one named last changes fastest.
Arguments:
- failed: int32 [64], P('dp'), may hold values from 0 to 15
- unfinished: int32 [64, 2], P('dp'), may hold values from 0 to 7, as said below
- lengths: int32 [64, 2], P('dp'), may hold values from 1 to 64
- acts: bfloat16 [16, 128, 64, 4096], P('section', 'dp'), may hold values from -100 to 100
- out_grads: bfloat16 [16, 512, 64, 512], P('section', 'dp'), may hold values from -30 to 30
- shadow_weight: bfloat16 [16, 4096, 512], P('section'), may hold values from -0.09375 to 0.09375
- shadow_gain: bfloat16 [16, 4096], P('section'), may hold values from 0.099609375 to 1.8984375
Outputs:
- in_grad: bfloat16 [16, 128, 64, 4096], P('section', 'dp')
- gain_grad: float32 [16, 4096], P('section', 'dp')
- bias_grad: float32 [16, 512], P('section', 'dp')
Inputs may be any that keep to these rules, and one draw needn't show every extreme that they name: `unfinished`: in each replica's row the 2 ids differ.
All inputs are finite; a program needn't handle non-finite values.
Results may differ from a plain program's by a relative error of at most 0.001.
Values may be sent and summed in bfloat16 or wider, within the bound.
No kernel may reach another device: no remote copies, remote signals or barrier semaphores. Data moves between devices by JAX's collectives and lax.ppermute only.
A program may use at most 32 MiB of HBM per device.

v0:
```python
import jax
import jax.numpy as jnp
from jax import lax
from jax.sharding import PartitionSpec as P

EPSILON = 1e-06


def passed_along(value, axis, steps):
    count = lax.axis_size(axis)
    pairs = [(source, (source + steps) % count) for source in range(count)]
    return lax.ppermute(value, axis, pairs)


def pick_live(block, picked_ids, live_len):
    chosen = jnp.take(block, picked_ids, axis=0)
    position = lax.broadcasted_iota(jnp.int32, chosen.shape[:2], 1)
    live = position < live_len[:, None]
    return jnp.where(live[..., None], chosen, jnp.zeros_like(chosen))


def local_backward(rows, grads, weight, gain, replicas):
    wide = rows.astype(jnp.float32)
    inv_rms = lax.rsqrt(jnp.mean(wide * wide, axis=1, keepdims=True) + EPSILON)
    normed = wide * inv_rms
    grad_norm = lax.dot_general(
        grads, weight, (((1,), (1,)), ((), ())), preferred_element_type=jnp.float32
    )
    grad_hat = grad_norm * gain.astype(jnp.float32)[None, :]
    inner = jnp.mean(grad_hat * normed, axis=1, keepdims=True)
    result = (inv_rms * (grad_hat - normed * inner)).astype(jnp.bfloat16)
    gain_part = jnp.sum(grad_norm * normed, axis=0) / replicas
    bias_part = jnp.sum(grads.astype(jnp.float32), axis=0) / replicas
    return (result, gain_part, bias_part)


def per_device(failed, unfinished, lengths, acts, out_grads, shadow_weight, shadow_gain):
    sections = lax.axis_size("section")
    replicas = lax.axis_size("dp")
    broken = failed[0]
    helper = (broken + sections - 1) % sections
    my_section = lax.axis_index("section")
    on_helper = my_section == helper
    picked_ids = unfinished[0]
    live_len = lengths[0]
    slot_count, seq_len, channels = (acts.shape[1], acts.shape[2], acts.shape[3])
    features = out_grads.shape[3]
    total_rows = slot_count * seq_len
    outgoing = out_grads[0]
    incoming = outgoing
    for step in range(2):
        incoming = passed_along(incoming, "section", -1)
    grads = pick_live(incoming, picked_ids, live_len)
    collected, gain_part, bias_part = local_backward(
        acts[0].reshape(total_rows, channels),
        grads.reshape(total_rows, features),
        shadow_weight[0],
        shadow_gain[0],
        replicas,
    )
    collected = jnp.where(on_helper, collected, jnp.zeros_like(collected))
    gain_part = jnp.where(on_helper, gain_part, jnp.zeros_like(gain_part))
    bias_part = jnp.where(on_helper, bias_part, jnp.zeros_like(bias_part))
    gain_share, bias_share = (
        lax.psum_scatter(gain_part, "dp", scatter_dimension=0, tiled=True),
        lax.psum_scatter(bias_part, "dp", scatter_dimension=0, tiled=True),
    )
    in_grad = collected.reshape(1, slot_count, seq_len, channels)
    return (in_grad, gain_share[None, :], bias_share[None, :])


def solution(mesh):
    in_specs = (
        P("dp"),
        P("dp", None),
        P("dp", None),
        P("section", "dp", None, None),
        P("section", "dp", None, None),
        P("section", None, None),
        P("section", None),
    )
    out_specs = (P("section", "dp", None, None), P("section", "dp"), P("section", "dp"))
    return jax.shard_map(
        per_device, mesh=mesh, in_specs=in_specs, out_specs=out_specs, check_vma=False
    )
```

profile of v0, /device:TPU:1, one launch (start us, length us, event | category | flops | bytes accessed | tf_op | source)
XLA Modules:
  0.0 328.5 jit_solution(1247159197729112550)
XLA Ops:
  0.6 0.0 copy-start
  0.6 9.6 %collective-permute-start = (bf16[8,64,512]{2,1,0:T(8,128)(2,1)}, bf16[8,64,512]{2,1,0:T(8,128)(2,1)S(1)}, u32[]{:S(2)}, u32[]{:S(2)}) collective-permute-start(bf16[8,64,512]{2,1,0:T(8,128)(2,1)} %bitcast.37), channel_id=1, source_target_pairs={{0,960},{64,0},{128,64},{192,128},{256,192},{320,256},{384,320},{4... | collective-permute-start | bytes 1572872 | tf_op jit(solution)/shard_map/ppermute | solution.py:12
  10.2 1.5 multiply_reduce_fusion.2
  12.4 1.3 dynamic-slice
  15.0 0.1 rsqrt.12
  15.1 0.7 mul.57
  15.8 0.7 fusion.3
  16.5 0.2 collective-permute-done
  16.7 6.6 %collective-permute-start.1 = (bf16[8,64,512]{2,1,0:T(8,128)(2,1)S(1)}, bf16[8,64,512]{2,1,0:T(8,128)(2,1)S(1)}, u32[]{:S(2)}, u32[]{:S(2)}) collective-permute-start(bf16[8,64,512]{2,1,0:T(8,128)(2,1)S(1)} %collective-permute-done), channel_id=1, source_target_pairs={{0,960},{64,0},{128,64},{192,128},{256,192},{320,256},{384,320},{4... | collective-permute-start | bytes 1572872 | tf_op jit(solution)/shard_map/ppermute | solution.py:12
  23.4 0.7 compare_and_fusion
  24.0 0.7 iota_compare_fusion
  24.7 6.4 %collective-permute-done.1 = bf16[8,64,512]{2,1,0:T(8,128)(2,1)S(1)} collective-permute-done((bf16[8,64,512]{2,1,0:T(8,128)(2,1)S(1)}, bf16[8,64,512]{2,1,0:T(8,128)(2,1)S(1)}, u32[]{:S(2)}, u32[]{:S(2)}) %collective-permute-start.1) | collective-permute-done | bytes 524320 | tf_op jit(solution)/shard_map/ppermute | solution.py:12
  31.1 0.6 gather_fusion
  31.7 0.1 convert_reduce_fusion
  31.8 0.0 copy-done
  31.8 3.8 %multiply_reduce_fusion = (f32[4096]{0:T(1024)S(1)}, f32[128]{0:T(128)S(1)}, f32[128,4096]{1,0:T(8,128)S(1)}) fusion(bf16[1,2,64,4096]{3,2,1,0:T(8,128)(2,1)S(1)} %copy-done, f32[128]{0:T(128)S(1)} %rsqrt.12, f32[4096]{0:T(1024)S(1)} %bitcast.35, bf16[128,512]{1,0:T(8,128)(2,1)S(1)} %bitcast.34, bf16[1,4096,512]{2,1,0:T(8,128)(2,1)} %param.12), kind=kOutput, calls=%fused_computation.4 | convolution fusion | flops 540536704 | bytes 7504896 | tf_op jit(solution)/shard_map/dot_general | solution.py:26
  35.7 290.1 %all-reduce.2 = (f32[4096]{0:T(1024)S(1)}, f32[512]{0:T(512)S(1)}) all-reduce(f32[4096]{0:T(1024)S(1)} %multiply_select_fusion, f32[512]{0:T(512)S(1)} %multiply_select_fusion.1), channel_id=2, replica_groups=mesh['section'=16,'dp'=64] {'dp'}, use_global_device_ids=true, to_apply=%region_3.4.clone | all-reduce | flops 4608 | bytes 36864
  325.7 0.6 dynamic-slice_bitcast_fusion.1
  326.3 0.6 dynamic-slice_bitcast_fusion
  326.9 1.6 fusion.2
  (5 shorter events, 0.0 us)
Async XLA Ops:
  0.6 31.2 %copy-start = (bf16[1,2,64,4096]{3,2,1,0:T(8,128)(2,1)S(1)}, bf16[1,2,64,4096]{3,2,1,0:T(8,128)(2,1)}, u32[]{:S(2)}) copy-start(bf16[1,2,64,4096]{3,2,1,0:T(8,128)(2,1)} %param.10) | copy-start | bytes 3145732
  0.6 16.1 %collective-permute-start = (bf16[8,64,512]{2,1,0:T(8,128)(2,1)}, bf16[8,64,512]{2,1,0:T(8,128)(2,1)S(1)}, u32[]{:S(2)}, u32[]{:S(2)}) collective-permute-start(bf16[8,64,512]{2,1,0:T(8,128)(2,1)} %bitcast.37), channel_id=1, source_target_pairs={{0,960},{64,0},{128,64},{192,128},{256,192},{320,256},{384,320},{4... | collective-permute-start | bytes 1572872 | tf_op jit(solution)/shard_map/ppermute | solution.py:12
  16.7 14.4 %collective-permute-start.1 = (bf16[8,64,512]{2,1,0:T(8,128)(2,1)S(1)}, bf16[8,64,512]{2,1,0:T(8,128)(2,1)S(1)}, u32[]{:S(2)}, u32[]{:S(2)}) collective-permute-start(bf16[8,64,512]{2,1,0:T(8,128)(2,1)S(1)} %collective-permute-done), channel_id=1, source_target_pairs={{0,960},{64,0},{128,64},{192,128},{256,192},{320,256},{384,320},{4... | collective-permute-start | bytes 1572872 | tf_op jit(solution)/shard_map/ppermute | solution.py:12
where the time goes:
time: 332 us; the launch traced here: 328 us
  blocking collectives  290 us (87%)
  starting transfers between devices  16.2 us (5%)
  waiting for transfers between devices  6.61 us (2%)
  other arithmetic  6.02 us (2%)
  matrix products  3.8 us (1%)
    unnamed x1, blocking collectives  290 us
    ppermute x2, starting transfers between devices, passed_along(): return lax.ppermute(value, axis, pairs)  16.2 us
  transfers between devices with their start and end apart: 2, of which 2 were waited for; matrix products, arithmetic and copies ran while one was open for 2% of the time, Pallas kernels for 0%

commit v1 on v0

v1 whole, which is shorter than its diff:
```python
import jax
import jax.numpy as jnp
from jax import lax
from jax.sharding import PartitionSpec as P

EPSILON = 1e-06


def local_backward(rows, grads, weight, gain, replicas):
    wide = rows.astype(jnp.float32)
    inv_rms = lax.rsqrt(jnp.mean(wide * wide, axis=1, keepdims=True) + EPSILON)
    normed = wide * inv_rms
    grad_norm = lax.dot_general(
        grads, weight, (((1,), (1,)), ((), ())), preferred_element_type=jnp.float32
    )
    grad_hat = grad_norm * gain.astype(jnp.float32)[None, :]
    inner = jnp.mean(grad_hat * normed, axis=1, keepdims=True)
    result = (inv_rms * (grad_hat - normed * inner)).astype(jnp.bfloat16)
    gain_part = jnp.sum(grad_norm * normed, axis=0) / replicas
    bias_part = jnp.sum(grads.astype(jnp.float32), axis=0) / replicas
    return (result, gain_part, bias_part)


def reduce_over_dp(parts):
    got = lax.all_to_all(parts, "dp", 0, 0, tiled=True)
    return jnp.sum(got, axis=0, keepdims=True)


def per_device(failed, unfinished, lengths, acts, out_grads, shadow_weight, shadow_gain):
    sections = lax.axis_size("section")
    replicas = lax.axis_size("dp")
    helper = (failed[0] + sections - 1) % sections
    on_helper = lax.axis_index("section") == helper
    picked_ids = unfinished[0]
    live_len = lengths[0]
    slot_count, seq_len, channels = acts.shape[1], acts.shape[2], acts.shape[3]
    features = out_grads.shape[3]
    total_rows = slot_count * seq_len
    chosen = jnp.take(out_grads[0], picked_ids, axis=0)
    position = lax.broadcasted_iota(jnp.int32, chosen.shape[:2], 1)
    chosen = jnp.where((position < live_len[:, None])[..., None], chosen, jnp.zeros_like(chosen))
    pairs = [(s, (s - 2) % sections) for s in range(sections)]
    grads = lax.ppermute(chosen, "section", pairs)
    collected, gain_part, bias_part = local_backward(
        acts[0].reshape(total_rows, channels),
        grads.reshape(total_rows, features),
        shadow_weight[0], shadow_gain[0], replicas)
    collected = jnp.where(on_helper, collected, jnp.zeros_like(collected))
    gain_part = jnp.where(on_helper, gain_part, jnp.zeros_like(gain_part))
    bias_part = jnp.where(on_helper, bias_part, jnp.zeros_like(bias_part))
    parts = jnp.concatenate([gain_part.reshape(replicas, -1), bias_part.reshape(replicas, -1)], axis=1)
    mine = reduce_over_dp(parts)
    gw = channels // replicas
    in_grad = collected.reshape(1, slot_count, seq_len, channels)
    return (in_grad, mine[:, :gw], mine[:, gw:])


def solution(mesh):
    in_specs = (P("dp"), P("dp", None), P("dp", None), P("section", "dp", None, None),
                P("section", "dp", None, None), P("section", None, None), P("section", None))
    out_specs = (P("section", "dp", None, None), P("section", "dp"), P("section", "dp"))
    return jax.shard_map(per_device, mesh=mesh, in_specs=in_specs, out_specs=out_specs, check_vma=False)
```

time: 332 us -> 54.3 us (0.16)
  blocking collectives: 290 us -> 0 us
  starting transfers between devices: 16.2 us -> 28.9 us
    unnamed x1 -> x0, blocking collectives: 290 us -> none
    all_to_all x0 -> x1, starting transfers between devices: none -> 22.2 us  [reduce_over_dp(): got = lax.all_to_all(parts, 'dp', 0, 0, tiled=True)]
    ppermute x2 -> x1, starting transfers between devices: 16.2 us -> 6.72 us  [per_device(): grads = lax.ppermute(chosen, 'section', pairs)]
    all_to_all x0 -> x1, waiting for transfers between devices: none -> 8.63 us  [reduce_over_dp(): got = lax.all_to_all(parts, 'dp', 0, 0, tiled=True)]
    ppermute x2 -> x1, waiting for transfers between devices: 6.61 us -> 0.01 us  [per_device(): grads = lax.ppermute(chosen, 'section', pairs)]
  transfers between devices with their start and end apart: 2 -> 2, of which waited for: 2 -> 1; matrix products, arithmetic and copies ran while one was open for 2% -> 10% of each run, Pallas kernels for 0% -> 0%
where the time goes in v1:
time: 54.3 us; the launch traced here: 53.9 us
  starting transfers between devices  28.9 us (53%)
  waiting for transfers between devices  8.63 us (16%)
  other arithmetic  8.5 us (16%)
  matrix products  5.06 us (9%)
  local copies, waits for them, and re-layouts  1.4 us (3%)
  between operations  1.4 us (3%)
    all_to_all x1, starting transfers between devices, reduce_over_dp(): got = lax.all_to_all(parts, 'dp', 0, 0, tiled=True)  22.2 us
    all_to_all x1, waiting for transfers between devices, reduce_over_dp(): got = lax.all_to_all(parts, 'dp', 0, 0, tiled=True)  8.63 us
    ppermute x1, starting transfers between devices, per_device(): grads = lax.ppermute(chosen, 'section', pairs)  6.72 us
    dot_general x1, matrix products, local_backward(): lax.dot_general(grads, weight, (((1,), (1,)), ((), ())), preferred_elemen...  5.06 us
    select_n x1, other arithmetic, per_device(): collected = jnp.where(on_helper, collected, jnp.zeros_like(collected))  3.16 us
    reduce_sum x1, other arithmetic, local_backward(): inv_rms = lax.rsqrt(jnp.mean(wide * wide, axis=1, keepdims=True) + EPSILON)  1.52 us
  transfers between devices with their start and end apart: 2, of which 1 were waited for; matrix products, arithmetic and copies ran while one was open for 10% of the time, Pallas kernels for 0%

profile of v1, /device:TPU:1, one launch (start us, length us, event | category | flops | bytes accessed | tf_op | source)
XLA Modules:
  0.0 53.9 jit_solution(2990299026621847157)
XLA Ops:
  0.6 0.0 copy-start
  0.6 0.0 copy-start.1
  0.7 0.8 %fusion.3 = s32[2]{0:T(128)S(1)} fusion(s32[1,2]{1,0:T(1,128)} %param.8), kind=kLoop, calls=%fused_computation.20 | loop fusion | flops 6 | bytes 16 | tf_op jit(solution)/shard_map/jit(_take)/jit(_where)/select_n | solution.py:39
  1.4 0.7 %compare_and_fusion = pred[2]{0:T(512)(128)(4,1)S(1)} fusion(s32[1,2]{1,0:T(1,128)} %param.8), kind=kLoop, calls=%fused_computation.17 | loop fusion | flops 12 | bytes 10 | tf_op jit(solution)/shard_map/jit(_take)/and | solution.py:39
  2.1 0.7 %iota_compare_fusion = pred[2,64]{1,0:T(4,128)(4,1)S(1)} fusion(s32[2]{0:T(128)} %bitcast.38), kind=kLoop, calls=%fused_computation.18 | loop fusion | flops 128 | bytes 136 | tf_op jit(solution)/shard_map/lt | solution.py:41
  2.8 0.0 copy-done
  2.8 0.6 %gather_fusion = bf16[2,64,512]{2,1,0:T(8,128)(2,1)S(1)} fusion(bf16[8,64,512]{2,1,0:T(8,128)(2,1)S(1)} %bitcast.31, s32[1024]{0:T(1024)S(1)} %pad_clamp_fusion), kind=kCustom, calls=%fused_computation | custom fusion | bytes 262152 | tf_op jit(solution)/shard_map/jit(_take)/gather | solution.py:39
  3.4 0.1 select_select_fusion
  3.5 6.7 %collective-permute-start = (bf16[2,64,512]{2,1,0:T(8,128)(2,1)S(1)}, bf16[2,64,512]{2,1,0:T(8,128)(2,1)S(1)}, u32[]{:S(2)}, u32[]{:S(2)}) collective-permute-start(bf16[2,64,512]{2,1,0:T(8,128)(2,1)S(1)} %select_select_fusion), channel_id=1, source_target_pairs={{0,896},{64,960},{128,0},{192,64},{256,128},{320,192},{384,256},{4... | collective-permute-start | bytes 393224 | tf_op jit(solution)/shard_map/ppermute | solution.py:43
  10.9 1.5 %multiply_reduce_fusion.2 = f32[2,64]{1,0:T(2,128)S(1)} fusion(bf16[1,2,64,4096]{3,2,1,0:T(8,128)(2,1)} %param.10), kind=kLoop, calls=%fused_computation.7 | loop fusion | flops 1572736 | bytes 1049088 | tf_op jit(solution)/shard_map/reduce_sum | solution.py:11
  12.4 0.1 rsqrt.12
  12.5 0.7 %mul.57 = f32[1,4096]{1,0:T(1,128)S(1)} convert(bf16[1,4096]{1,0:T(2,128)(2,1)} %param.13) | non-fusion elementwise | flops 4096 | bytes 24576 | tf_op jit(solution)/shard_map/mul | solution.py:16
  13.3 0.0 collective-permute-done
  13.3 0.1 select_n.75
  13.4 0.0 copy-done.1
  13.4 5.1 %multiply_reduce_fusion = (f32[4096]{0:T(1024)S(1)}, f32[128]{0:T(128)S(1)}, f32[128,4096]{1,0:T(8,128)}) fusion(bf16[1,2,64,4096]{3,2,1,0:T(8,128)(2,1)S(1)} %copy-done.1, f32[128]{0:T(128)S(1)} %rsqrt.12, f32[4096]{0:T(1024)S(1)} %bitcast.34, bf16[128,512]{1,0:T(8,128)(2,1)S(1)} %bitcast.33, bf16[1,4096,512]{2,1,0:T(8,128)(2,1)} %param.12), kind=kOutput, calls=%fused_computation.4 | convolution fusion | flops 540536704 | bytes 7504896 | tf_op jit(solution)/shard_map/dot_general | solution.py:13
  18.5 0.1 select_n.72
  18.6 0.7 %pad_maximum_fusion = f32[64,72]{1,0:T(8,128)} fusion(f32[64,8]{1,0:T(8,128)S(1)} %select_n.75, f32[64,64]{1,0:T(8,128)S(1)} %select_n.72), kind=kLoop, calls=%fused_computation.11 | loop fusion | flops 4608 | bytes 36864 | tf_op jit(solution)/shard_map/concatenate | solution.py:51
  19.2 22.2 %all-to-all-start = ((f32[64,1,72]{2,1,0:T(1,128)}), f32[64,1,72]{2,1,0:T(1,128)S(1)}, u32[]{:S(2)}, u32[]{:S(2)}) async-start(f32[64,1,72]{2,1,0:T(1,128)} %bitcast.11), calls=%async_computation | async-start | bytes 65536 | tf_op jit(solution)/shard_map/all_to_all | solution.py:25
  41.4 3.2 %fusion.2 = bf16[128,4096]{1,0:T(8,128)(2,1)} fusion(bf16[1,2,64,4096]{3,2,1,0:T(8,128)(2,1)S(1)} %copy-done.1, f32[128,4096]{1,0:T(8,128)} %get-tuple-element.5, f32[128]{0:T(128)S(1)} %broadcast_multiply_fusion, f32[4096]{0:T(1024)S(1)} %bitcast.35, f32[128]{0:T(128)S(1)} %rsqrt.12, pred[]{:T(512)S(6)} %eq.5), kind=kLoop, calls=%fused_computation.8 | loop fusion | flops 4194304 | bytes 4211713 | tf_op jit(solution)/shard_map/jit(_where)/select_n | solution.py:48
  44.6 8.6 %all-to-all-done = f32[64,1,72]{2,1,0:T(1,128)S(1)} async-done(((f32[64,1,72]{2,1,0:T(1,128)}), f32[64,1,72]{2,1,0:T(1,128)S(1)}, u32[]{:S(2)}, u32[]{:S(2)}) %all-to-all-start) | async-done | bytes 18464 | tf_op jit(solution)/shard_map/all_to_all | solution.py:25
  53.2 0.1 reduce_sum.49
  53.3 0.0 copy-start.2
  53.3 0.6 %slice.7 = f32[1,8]{1,0:T(1,128)} slice(f32[1,72]{1,0:T(1,128)S(1)} %bitcast.36), slice={[0:1], [64:72]} | slice | bytes 64 | tf_op jit(solution)/shard_map/slice | solution.py:55
  53.9 0.0 copy-done.2
  (6 shorter events, 0.1 us)
Async XLA Ops:
  0.6 2.2 %copy-start = (bf16[1,8,64,512]{3,2,1,0:T(8,128)(2,1)S(1)}, bf16[1,8,64,512]{3,2,1,0:T(8,128)(2,1)}, u32[]{:S(2)}) copy-start(bf16[1,8,64,512]{3,2,1,0:T(8,128)(2,1)} %param.11) | copy-start | bytes 1572868
  0.6 12.8 %copy-start.1 = (bf16[1,2,64,4096]{3,2,1,0:T(8,128)(2,1)S(1)}, bf16[1,2,64,4096]{3,2,1,0:T(8,128)(2,1)}, u32[]{:S(2)}) copy-start(bf16[1,2,64,4096]{3,2,1,0:T(8,128)(2,1)} %param.10) | copy-start | bytes 3145732
  3.5 9.8 %collective-permute-start = (bf16[2,64,512]{2,1,0:T(8,128)(2,1)S(1)}, bf16[2,64,512]{2,1,0:T(8,128)(2,1)S(1)}, u32[]{:S(2)}, u32[]{:S(2)}) collective-permute-start(bf16[2,64,512]{2,1,0:T(8,128)(2,1)S(1)} %select_select_fusion), channel_id=1, source_target_pairs={{0,896},{64,960},{128,0},{192,64},{256,128},{320,192},{384,256},{4... | collective-permute-start | bytes 393224 | tf_op jit(solution)/shard_map/ppermute | solution.py:43
  19.2 34.0 %all-to-all-start = ((f32[64,1,72]{2,1,0:T(1,128)}), f32[64,1,72]{2,1,0:T(1,128)S(1)}, u32[]{:S(2)}, u32[]{:S(2)}) async-start(f32[64,1,72]{2,1,0:T(1,128)} %bitcast.11), calls=%async_computation | async-start | bytes 65536 | tf_op jit(solution)/shard_map/all_to_all | solution.py:25
  53.3 0.6 %copy-start.2 = (f32[72]{0:T(128)}, f32[72]{0:T(128)S(1)}, u32[]{:S(2)}) copy-start(f32[72]{0:T(128)S(1)} %reduce_sum.49) | copy-start | bytes 868

commit v2 on v1

v2 whole, which is shorter than its diff:
```python
import jax
import jax.numpy as jnp
from jax import lax
from jax.experimental import pallas as pl
from jax.experimental.pallas import tpu as pltpu
from jax.sharding import PartitionSpec as P

EPSILON = 1e-06
BLOCK = 512


def terms_kernel(g_ref, keep_ref, a_ref, r_ref, w_ref, gain_ref, bias_ref):
    g = jnp.where(keep_ref[...] > 0, g_ref[...], jnp.zeros_like(g_ref[...]))
    bias_ref[...] = jnp.sum(g.astype(jnp.float32), axis=0, keepdims=True)
    inv_rms = r_ref[...]
    for j in range(a_ref.shape[1] // BLOCK):
        cols = slice(j * BLOCK, (j + 1) * BLOCK)
        grad_norm = lax.dot_general(
            g, w_ref[cols, :], (((1,), (1,)), ((), ())), preferred_element_type=jnp.float32
        )
        normed = a_ref[:, cols].astype(jnp.float32) * inv_rms
        gain_ref[:, cols] = jnp.sum(grad_norm * normed, axis=0, keepdims=True)


def reduction_terms(grads, keep, rows, inv_rms, weight):
    tokens, features = grads.shape
    channels = rows.shape[1]
    vmem = pl.BlockSpec(memory_space=pltpu.VMEM)
    return pl.pallas_call(
        terms_kernel,
        out_shape=(
            jax.ShapeDtypeStruct((1, channels), jnp.float32),
            jax.ShapeDtypeStruct((1, features), jnp.float32),
        ),
        in_specs=[vmem] * 5,
        out_specs=(vmem, vmem),
        cost_estimate=pl.CostEstimate(
            flops=2 * tokens * features * channels,
            bytes_accessed=2 * (channels * features + tokens * channels + tokens * features),
            transcendentals=0,
        ),
    )(grads, keep, rows, inv_rms, weight)


def per_device(failed, unfinished, lengths, acts, out_grads, shadow_weight, shadow_gain):
    sections = lax.axis_size("section")
    replicas = lax.axis_size("dp")
    helper = (failed[0] + sections - 1) % sections
    on_helper = lax.axis_index("section") == helper
    picked_ids = unfinished[0]
    live_len = lengths[0]
    slot_count, seq_len, channels = acts.shape[1], acts.shape[2], acts.shape[3]
    features = out_grads.shape[3]
    total_rows = slot_count * seq_len

    chosen = jnp.take(out_grads[0], picked_ids, axis=0)
    pairs = [(s, (s - 2) % sections) for s in range(sections)]
    grads = lax.ppermute(chosen, "section", pairs).reshape(total_rows, features)
    position = lax.broadcasted_iota(jnp.int32, (slot_count, seq_len), 1)
    live = (position < live_len[:, None]).reshape(total_rows, 1)

    rows = acts[0].reshape(total_rows, channels)
    wide = rows.astype(jnp.float32)
    inv_rms = lax.rsqrt(jnp.mean(wide * wide, axis=1, keepdims=True) + EPSILON)
    weight = shadow_weight[0]

    gain_sum, bias_sum = reduction_terms(grads, live.astype(jnp.float32), rows, inv_rms, weight)
    gain_part = jnp.where(on_helper, gain_sum / replicas, 0.0)
    bias_part = jnp.where(on_helper, bias_sum / replicas, 0.0)
    parts = jnp.concatenate(
        [gain_part.reshape(replicas, -1), bias_part.reshape(replicas, -1)], axis=1
    )
    mine = jnp.sum(lax.all_to_all(parts, "dp", 0, 0, tiled=True), axis=0, keepdims=True)

    masked = jnp.where(live, grads, jnp.zeros_like(grads))
    normed = wide * inv_rms
    grad_norm = lax.dot_general(
        masked, weight, (((1,), (1,)), ((), ())), preferred_element_type=jnp.float32
    )
    grad_hat = grad_norm * shadow_gain[0].astype(jnp.float32)[None, :]
    inner = jnp.mean(grad_hat * normed, axis=1, keepdims=True)
    dx = (inv_rms * (grad_hat - normed * inner)).astype(jnp.bfloat16)
    dx = jnp.where(on_helper, dx, jnp.zeros_like(dx))

    width = channels // replicas
    in_grad = dx.reshape(1, slot_count, seq_len, channels)
    return (in_grad, mine[:, :width], mine[:, width:])


def solution(mesh):
    in_specs = (
        P("dp"),
        P("dp", None),
        P("dp", None),
        P("section", "dp", None, None),
        P("section", "dp", None, None),
        P("section", None, None),
        P("section", None),
    )
    out_specs = (P("section", "dp", None, None), P("section", "dp"), P("section", "dp"))
    return jax.shard_map(
        per_device, mesh=mesh, in_specs=in_specs, out_specs=out_specs, check_vma=False
    )
```

time: 54.3 us -> 57.6 us (1.061)
  Pallas kernels: 0 us -> 4.84 us
  waiting for transfers between devices: 8.63 us -> 5.49 us
  local copies, waits for them, and re-layouts: 1.4 us -> 3.56 us
  matrix products: 5.06 us -> 3.76 us
  other arithmetic: 8.5 us -> 9.21 us
    pallas_call x0 -> x1, Pallas kernels: none -> 4.84 us  [reduction_terms(): pl.pallas_call(terms_kernel, out_shape=(jax.ShapeDtypeStruct((1, channels...]
    all_to_all x1, waiting for transfers between devices: 8.63 us -> 5.49 us  [per_device(): lax.all_to_all(parts, 'dp', 0, 0, tiled=True)]
    dot_general x1, matrix products: 5.06 us -> 3.76 us  [per_device(): lax.dot_general(masked, weight, (((1,), (1,)), ((), ())), preferred_eleme...]
    rsqrt x1 -> x2, local copies, waits for them, and re-layouts: 0.08 us -> 0.84 us  [per_device(): inv_rms = lax.rsqrt(jnp.mean(wide * wide, axis=1, keepdims=True) + EPSILON)]
    convert_element_type x0 -> x1, local copies, waits for them, and re-layouts: none -> 0.76 us  [per_device(): live.astype(jnp.float32)]
    convert_element_type x0 -> x1, other arithmetic: none -> 0.73 us  [per_device(): live.astype(jnp.float32)]
    lt x1 -> x0, other arithmetic: 0.73 us -> none  [per_device(): position < live_len[:, None]]
    select_n x4, other arithmetic: 3.26 us -> 3.98 us  [the longest x1 1.51 us: per_device(): dx = jnp.where(on_helper, dx, jnp.zeros_like(dx))]
  transfers between devices with their start and end apart: 2 -> 2, of which waited for: 1 -> 1; matrix products, arithmetic and copies ran while one was open for 10% -> 19% of each run, Pallas kernels for 0% -> 0%
where the time goes in v2:
time: 57.6 us; the launch traced here: 57.2 us
  starting transfers between devices  28.9 us (50%)
  other arithmetic  9.21 us (16%)
  waiting for transfers between devices  5.49 us (10%)
  Pallas kernels  4.84 us (8%)
  matrix products  3.76 us (7%)
  local copies, waits for them, and re-layouts  3.56 us (6%)
  between operations  1.39 us (2%)
    all_to_all x1, starting transfers between devices, per_device(): lax.all_to_all(parts, 'dp', 0, 0, tiled=True)  22.2 us
    ppermute x1, starting transfers between devices, per_device(): grads = lax.ppermute(chosen, 'section', pairs).reshape(total_rows, features)  6.72 us
    all_to_all x1, waiting for transfers between devices, per_device(): lax.all_to_all(parts, 'dp', 0, 0, tiled=True)  5.49 us
    pallas_call x1, Pallas kernels, reduction_terms(): pl.pallas_call(terms_kernel, out_shape=(jax.ShapeDtypeStruct((1, channels...  4.84 us
    dot_general x1, matrix products, per_device(): lax.dot_general(masked, weight, (((1,), (1,)), ((), ())), preferred_eleme...  3.76 us
    reduce_sum x1, other arithmetic, per_device(): inv_rms = lax.rsqrt(jnp.mean(wide * wide, axis=1, keepdims=True) + EPSILON)  1.52 us
    select_n x1, other arithmetic, per_device(): dx = jnp.where(on_helper, dx, jnp.zeros_like(dx))  1.51 us
  transfers between devices with their start and end apart: 2, of which 1 were waited for; matrix products, arithmetic and copies ran while one was open for 19% of the time, Pallas kernels for 0%

profile of v2, /device:TPU:1, one launch (start us, length us, event | category | flops | bytes accessed | tf_op | source)
XLA Modules:
  0.0 57.2 jit_solution(17605653307215599970)
XLA Ops:
  0.6 0.0 copy-start
  0.6 0.7 %fusion.3 = s32[2]{0:T(128)S(1)} fusion(s32[1,2]{1,0:T(1,128)} %param.8), kind=kLoop, calls=%fused_computation.20 | loop fusion | flops 6 | bytes 16 | tf_op jit(solution)/shard_map/jit(_take)/jit(_where)/select_n | solution.py:56
  1.4 0.7 %compare_and_fusion = pred[2]{0:T(512)(128)(4,1)S(1)} fusion(s32[1,2]{1,0:T(1,128)} %param.8), kind=kLoop, calls=%fused_computation.17 | loop fusion | flops 12 | bytes 10 | tf_op jit(solution)/shard_map/jit(_take)/and | solution.py:56
  2.0 0.0 copy-done
  2.0 0.6 gather_fusion
  2.6 0.1 broadcast_select_fusion
  2.7 6.7 %collective-permute-start = (bf16[2,64,512]{2,1,0:T(8,128)(2,1)S(1)}, bf16[2,64,512]{2,1,0:T(8,128)(2,1)S(1)}, u32[]{:S(2)}, u32[]{:S(2)}) collective-permute-start(bf16[2,64,512]{2,1,0:T(8,128)(2,1)S(1)} %broadcast_select_fusion), channel_id=1, source_target_pairs={{0,896},{64,960},{128,0},{192,64},{256,128},{320,192},{384,256},{4... | collective-permute-start | bytes 393224 | tf_op jit(solution)/shard_map/ppermute | solution.py:58
  10.1 1.5 %multiply_reduce_fusion.1 = f32[2,64]{1,0:T(2,128)S(1)} fusion(bf16[1,2,64,4096]{3,2,1,0:T(8,128)(2,1)} %param.10), kind=kLoop, calls=%fused_computation.5 | loop fusion | flops 1572736 | bytes 1049088 | tf_op jit(solution)/shard_map/reduce_sum | solution.py:64
  11.6 0.1 rsqrt.8
  11.7 0.8 %rsqrt.10.r_ref = f32[128,1]{1,0:T(8,128)} reshape(f32[2,64]{1,0:T(2,128)S(1)} %add_rsqrt_fusion) | data formatting | bytes 1024 | tf_op jit(solution)/shard_map/rsqrt | solution.py:64
  12.5 0.7 %mul.53 = f32[1,4096]{1,0:T(1,128)S(1)} convert(bf16[1,4096]{1,0:T(2,128)(2,1)} %param.13) | non-fusion elementwise | flops 4096 | bytes 24576 | tf_op jit(solution)/shard_map/mul | solution.py:80
  13.2 0.7 %fusion.5 = (f32[2,64]{1,0:T(2,128)S(1)}, pred[2,64]{1,0:T(4,128)(4,1)S(1)}) fusion(s32[2]{0:T(128)} %bitcast.34), kind=kLoop, calls=%fused_computation.23 | loop fusion | flops 256 | bytes 648 | tf_op jit(solution)/shard_map/convert_element_type | solution.py:67
  13.9 0.8 %reshape.149.keep_ref = f32[128,1]{1,0:T(8,128)} reshape(f32[2,64]{1,0:T(2,128)S(1)} %get-tuple-element.7) | data formatting | bytes 1024 | tf_op jit(solution)/shard_map/convert_element_type | solution.py:67
  14.7 0.0 collective-permute-done
  14.7 0.0 copy-start.2
  14.7 0.7 %copy-done.2 = bf16[2,64,512]{2,1,0:T(8,128)(2,1)} copy-done((bf16[2,64,512]{2,1,0:T(8,128)(2,1)}, bf16[2,64,512]{2,1,0:T(8,128)(2,1)S(1)}, u32[]{:S(2)}) %copy-start.2) | copy-done | bytes 131096
  15.3 0.0 copy-start.1
  15.4 4.8 %shard_map.94 = (f32[1,4096]{1,0:T(1,128)}, f32[1,512]{1,0:T(1,128)}) custom-call(bf16[128,512]{1,0:T(8,128)(2,1)} %bitcast.30, f32[128,1]{1,0:T(8,128)} %reshape.149.keep_ref, bf16[128,4096]{1,0:T(8,128)(2,1)} %bitcast.27, f32[128,1]{1,0:T(8,128)} %rsqrt.10.r_ref, bf16[4096,512]{1,0:T(8,128)(2,1)} %bitcast.26), custom_call_target="tpu_custom_call" | custom-call | flops 536870912 | bytes 5373952 | tf_op jit(solution)/shard_map/pallas_call | solution.py:29
  20.2 0.8 %fusion.1 = f32[4096]{0:T(1024)S(1)} fusion(pred[]{:T(512)S(6)} %eq.5, f32[1,4096]{1,0:T(1,128)} %get-tuple-element.5), kind=kLoop, calls=%fused_computation.11 | loop fusion | flops 8192 | bytes 32769 | tf_op jit(solution)/shard_map/jit(_where)/select_n | solution.py:68
  21.0 0.7 %fusion.2 = f32[512]{0:T(512)S(1)} fusion(pred[]{:T(512)S(6)} %eq.5, f32[1,512]{1,0:T(1,128)} %get-tuple-element.6), kind=kLoop, calls=%fused_computation.16 | loop fusion | flops 1024 | bytes 4097 | tf_op jit(solution)/shard_map/jit(_where)/select_n | solution.py:69
  21.7 0.1 reshape.137
  21.7 0.1 reshape.138
  21.8 0.7 %pad_maximum_fusion = f32[64,72]{1,0:T(8,128)} fusion(f32[64,8]{1,0:T(8,128)S(1)} %reshape.138, f32[64,64]{1,0:T(8,128)S(1)} %reshape.137), kind=kLoop, calls=%fused_computation.9 | loop fusion | flops 4608 | bytes 36864 | tf_op jit(solution)/shard_map/concatenate | solution.py:70
  22.5 22.2 %all-to-all-start = ((f32[64,1,72]{2,1,0:T(1,128)}), f32[64,1,72]{2,1,0:T(1,128)S(1)}, u32[]{:S(2)}, u32[]{:S(2)}) async-start(f32[64,1,72]{2,1,0:T(1,128)} %bitcast.12), calls=%async_computation | async-start | bytes 65536 | tf_op jit(solution)/shard_map/all_to_all | solution.py:73
  44.7 1.0 %broadcast_select_fusion.1 = bf16[2,64,512]{2,1,0:T(8,128)(2,1)S(1)} fusion(bf16[2,64,512]{2,1,0:T(8,128)(2,1)} %copy-done.2, pred[2,64]{1,0:T(4,128)(4,1)S(1)} %get-tuple-element.8), kind=kLoop, calls=%fused_computation.8 | loop fusion | flops 65536 | bytes 262272 | tf_op jit(solution)/shard_map/jit(_where)/select_n | solution.py:75
  45.7 0.0 copy-done.1
  45.7 3.8 %multiply_reduce_fusion = (f32[128]{0:T(128)S(1)}, f32[128,4096]{1,0:T(8,128)S(1)}) fusion(f32[128]{0:T(128)S(1)} %rsqrt.8, bf16[1,2,64,4096]{3,2,1,0:T(8,128)(2,1)S(1)} %copy-done.1, f32[4096]{0:T(1024)S(1)} %bitcast.31, bf16[128,512]{1,0:T(8,128)(2,1)S(1)} %bitcast.29, bf16[1,4096,512]{2,1,0:T(8,128)(2,1)} %param.12), kind=kOutput, calls=%fused_computation.3 | convolution fusion | flops 539492224 | bytes 7488512 | tf_op jit(solution)/shard_map/dot_general | solution.py:77
  49.5 1.5 %fusion = bf16[128,4096]{1,0:T(8,128)(2,1)} fusion(f32[128,4096]{1,0:T(8,128)S(1)} %get-tuple-element.10, f32[128]{0:T(128)S(1)} %broadcast_multiply_fusion, f32[128]{0:T(128)S(1)} %rsqrt.8, pred[]{:T(512)S(6)} %eq.5, bf16[1,2,64,4096]{3,2,1,0:T(8,128)(2,1)S(1)} %copy-done.1), kind=kLoop, calls=%fused_computation.6 | loop fusion | flops 3670016 | bytes 4195329 | tf_op jit(solution)/shard_map/jit(_where)/select_n | solution.py:83
  51.0 5.5 %all-to-all-done = f32[64,1,72]{2,1,0:T(1,128)S(1)} async-done(((f32[64,1,72]{2,1,0:T(1,128)}), f32[64,1,72]{2,1,0:T(1,128)S(1)}, u32[]{:S(2)}, u32[]{:S(2)}) %all-to-all-start) | async-done | bytes 18464 | tf_op jit(solution)/shard_map/all_to_all | solution.py:73
  56.5 0.1 reduce_sum.29
  56.6 0.0 copy-start.3
  56.6 0.6 %slice.7 = f32[1,8]{1,0:T(1,128)} slice(f32[1,72]{1,0:T(1,128)S(1)} %bitcast.32), slice={[0:1], [64:72]} | slice | bytes 64 | tf_op jit(solution)/shard_map/slice | solution.py:87
  57.2 0.0 copy-done.3
  (3 shorter events, 0.0 us)
Async XLA Ops:
  0.6 1.4 %copy-start = (bf16[1,8,64,512]{3,2,1,0:T(8,128)(2,1)S(1)}, bf16[1,8,64,512]{3,2,1,0:T(8,128)(2,1)}, u32[]{:S(2)}) copy-start(bf16[1,8,64,512]{3,2,1,0:T(8,128)(2,1)} %param.11) | copy-start | bytes 1572868
  2.7 12.0 %collective-permute-start = (bf16[2,64,512]{2,1,0:T(8,128)(2,1)S(1)}, bf16[2,64,512]{2,1,0:T(8,128)(2,1)S(1)}, u32[]{:S(2)}, u32[]{:S(2)}) collective-permute-start(bf16[2,64,512]{2,1,0:T(8,128)(2,1)S(1)} %broadcast_select_fusion), channel_id=1, source_target_pairs={{0,896},{64,960},{128,0},{192,64},{256,128},{320,192},{384,256},{4... | collective-permute-start | bytes 393224 | tf_op jit(solution)/shard_map/ppermute | solution.py:58
  14.7 0.7 %copy-start.2 = (bf16[2,64,512]{2,1,0:T(8,128)(2,1)}, bf16[2,64,512]{2,1,0:T(8,128)(2,1)S(1)}, u32[]{:S(2)}) copy-start(bf16[2,64,512]{2,1,0:T(8,128)(2,1)S(1)} %collective-permute-done) | copy-start | bytes 393220
  15.3 30.4 %copy-start.1 = (bf16[1,2,64,4096]{3,2,1,0:T(8,128)(2,1)S(1)}, bf16[1,2,64,4096]{3,2,1,0:T(8,128)(2,1)}, u32[]{:S(2)}) copy-start(bf16[1,2,64,4096]{3,2,1,0:T(8,128)(2,1)} %param.10) | copy-start | bytes 3145732
  22.5 34.0 %all-to-all-start = ((f32[64,1,72]{2,1,0:T(1,128)}), f32[64,1,72]{2,1,0:T(1,128)S(1)}, u32[]{:S(2)}, u32[]{:S(2)}) async-start(f32[64,1,72]{2,1,0:T(1,128)} %bitcast.12), calls=%async_computation | async-start | bytes 65536 | tf_op jit(solution)/shard_map/all_to_all | solution.py:73
  56.6 0.6 %copy-start.3 = (f32[72]{0:T(128)}, f32[72]{0:T(128)S(1)}, u32[]{:S(2)}) copy-start(f32[72]{0:T(128)S(1)} %reduce_sum.29) | copy-start | bytes 868

commit v3 on v1

--- a/solution.py
+++ b/solution.py
@@ -36,11 +36,11 @@
     slot_count, seq_len, channels = acts.shape[1], acts.shape[2], acts.shape[3]
     features = out_grads.shape[3]
     total_rows = slot_count * seq_len
-    chosen = jnp.take(out_grads[0], picked_ids, axis=0)
-    position = lax.broadcasted_iota(jnp.int32, chosen.shape[:2], 1)
-    chosen = jnp.where((position < live_len[:, None])[..., None], chosen, jnp.zeros_like(chosen))
+    chosen = jnp.take(out_grads[0], picked_ids, axis=0, mode="clip")
     pairs = [(s, (s - 2) % sections) for s in range(sections)]
     grads = lax.ppermute(chosen, "section", pairs)
+    position = lax.broadcasted_iota(jnp.int32, grads.shape[:2], 1)
+    grads = jnp.where((position < live_len[:, None])[..., None], grads, jnp.zeros_like(grads))
     collected, gain_part, bias_part = local_backward(
         acts[0].reshape(total_rows, channels),
         grads.reshape(total_rows, features),

time: 54.3 us -> 53.8 us (level)
  other arithmetic: 8.5 us -> 7.82 us
    select_n x2 -> x0, other arithmetic: 0.86 us -> none  [the longest x1 0.78 us: per_device(): chosen = jnp.take(out_grads[0], picked_ids, axis=0)]
    gather x1, other arithmetic: 0.01 us -> 0.78 us  [per_device(): chosen = jnp.take(out_grads[0], picked_ids, axis=0, mode='clip')]
    and x1 -> x0, other arithmetic: 0.66 us -> none  [per_device(): chosen = jnp.take(out_grads[0], picked_ids, axis=0)]
  transfers between devices with their start and end apart: 2 -> 2, of which waited for: 1 -> 1; matrix products, arithmetic and copies ran while one was open for 10% -> 12% of each run, Pallas kernels for 0% -> 0%
where the time goes in v3:
time: 53.8 us; the launch traced here: 53.4 us
  starting transfers between devices  28.9 us (54%)
  waiting for transfers between devices  8.62 us (16%)
  other arithmetic  7.82 us (15%)
  matrix products  5.06 us (9%)
  local copies, waits for them, and re-layouts  1.66 us (3%)
  between operations  1.37 us (3%)
    all_to_all x1, starting transfers between devices, reduce_over_dp(): got = lax.all_to_all(parts, 'dp', 0, 0, tiled=True)  22.2 us
    all_to_all x1, waiting for transfers between devices, reduce_over_dp(): got = lax.all_to_all(parts, 'dp', 0, 0, tiled=True)  8.62 us
    ppermute x1, starting transfers between devices, per_device(): grads = lax.ppermute(chosen, 'section', pairs)  6.72 us
    dot_general x1, matrix products, local_backward(): lax.dot_general(grads, weight, (((1,), (1,)), ((), ())), preferred_elemen...  5.06 us
    select_n x1, other arithmetic, per_device(): collected = jnp.where(on_helper, collected, jnp.zeros_like(collected))  3.16 us
    reduce_sum x1, other arithmetic, local_backward(): inv_rms = lax.rsqrt(jnp.mean(wide * wide, axis=1, keepdims=True) + EPSILON)  1.52 us
  transfers between devices with their start and end apart: 2, of which 1 were waited for; matrix products, arithmetic and copies ran while one was open for 12% of the time, Pallas kernels for 0%

profile of v3, /device:TPU:1, one launch (start us, length us, event | category | flops | bytes accessed | tf_op | source)
XLA Modules:
  0.0 53.4 jit_solution(5299985351234230729)
XLA Ops:
  0.6 0.0 copy-start
  0.6 0.0 copy-start.1
  0.7 0.8 %pad_clamp_fusion = s32[1024]{0:T(1024)S(1)} fusion(s32[2]{0:T(128)} %bitcast.33), kind=kLoop, calls=%fused_computation.13 | loop fusion | flops 1024 | bytes 4104 | tf_op jit(solution)/shard_map/jit(_take)/gather | solution.py:39
  1.4 0.3 copy-done
  1.7 0.6 %gather_fusion = bf16[2,64,512]{2,1,0:T(8,128)(2,1)S(1)} fusion(bf16[8,64,512]{2,1,0:T(8,128)(2,1)S(1)} %bitcast.26, s32[1024]{0:T(1024)S(1)} %pad_clamp_fusion), kind=kCustom, calls=%fused_computation | custom fusion | bytes 262152 | tf_op jit(solution)/shard_map/jit(_take)/gather | solution.py:39
  2.3 6.7 %collective-permute-start = (bf16[2,64,512]{2,1,0:T(8,128)(2,1)S(1)}, bf16[2,64,512]{2,1,0:T(8,128)(2,1)S(1)}, u32[]{:S(2)}, u32[]{:S(2)}) collective-permute-start(bf16[2,64,512]{2,1,0:T(8,128)(2,1)S(1)} %gather_fusion), channel_id=1, source_target_pairs={{0,896},{64,960},{128,0},{192,64},{256,128},{320,192},{384,256},{4... | collective-permute-start | bytes 393224 | tf_op jit(solution)/shard_map/ppermute | solution.py:41
  9.7 0.7 %mul.57 = f32[1,4096]{1,0:T(1,128)S(1)} convert(bf16[1,4096]{1,0:T(2,128)(2,1)} %param.13) | non-fusion elementwise | flops 4096 | bytes 24576 | tf_op jit(solution)/shard_map/mul | solution.py:16
  10.4 1.5 %multiply_reduce_fusion.2 = f32[2,64]{1,0:T(2,128)S(1)} fusion(bf16[1,2,64,4096]{3,2,1,0:T(8,128)(2,1)} %param.10), kind=kLoop, calls=%fused_computation.7 | loop fusion | flops 1572736 | bytes 1049088 | tf_op jit(solution)/shard_map/reduce_sum | solution.py:11
  11.9 0.1 rsqrt.12
  12.0 0.7 %iota_compare_fusion = pred[2,64]{1,0:T(4,128)(4,1)S(1)} fusion(s32[2]{0:T(128)} %bitcast.34), kind=kLoop, calls=%fused_computation.15 | loop fusion | flops 128 | bytes 136 | tf_op jit(solution)/shard_map/lt | solution.py:43
  12.7 0.0 collective-permute-done
  12.7 0.1 convert_reduce_fusion
  12.9 0.0 copy-done.1
  12.9 5.1 %multiply_reduce_fusion = (f32[4096]{0:T(1024)S(1)}, f32[128]{0:T(128)S(1)}, f32[128,4096]{1,0:T(8,128)}) fusion(bf16[1,2,64,4096]{3,2,1,0:T(8,128)(2,1)S(1)} %copy-done.1, f32[128]{0:T(128)S(1)} %rsqrt.12, f32[4096]{0:T(1024)S(1)} %bitcast.29, bf16[128,512]{1,0:T(8,128)(2,1)S(1)} %bitcast.28, bf16[1,4096,512]{2,1,0:T(8,128)(2,1)} %param.12), kind=kOutput, calls=%fused_computation.4 | convolution fusion | flops 540536704 | bytes 7504896 | tf_op jit(solution)/shard_map/dot_general | solution.py:13
  17.9 0.1 select_n.49
  18.0 0.1 select_n.52
  18.1 0.7 %pad_maximum_fusion = f32[64,72]{1,0:T(8,128)} fusion(f32[64,8]{1,0:T(8,128)S(1)} %select_n.52, f32[64,64]{1,0:T(8,128)S(1)} %select_n.49), kind=kLoop, calls=%fused_computation.11 | loop fusion | flops 4608 | bytes 36864 | tf_op jit(solution)/shard_map/concatenate | solution.py:51
  18.8 22.2 %all-to-all-start = ((f32[64,1,72]{2,1,0:T(1,128)}), f32[64,1,72]{2,1,0:T(1,128)S(1)}, u32[]{:S(2)}, u32[]{:S(2)}) async-start(f32[64,1,72]{2,1,0:T(1,128)} %bitcast.9), calls=%async_computation | async-start | bytes 65536 | tf_op jit(solution)/shard_map/all_to_all | solution.py:25
  41.0 3.2 %fusion.2 = bf16[128,4096]{1,0:T(8,128)(2,1)} fusion(bf16[1,2,64,4096]{3,2,1,0:T(8,128)(2,1)S(1)} %copy-done.1, f32[128,4096]{1,0:T(8,128)} %get-tuple-element.7, f32[128]{0:T(128)S(1)} %broadcast_multiply_fusion, f32[4096]{0:T(1024)S(1)} %bitcast.30, f32[128]{0:T(128)S(1)} %rsqrt.12, pred[]{:T(512)S(6)} %eq.5), kind=kLoop, calls=%fused_computation.8 | loop fusion | flops 4194304 | bytes 4211713 | tf_op jit(solution)/shard_map/jit(_where)/select_n | solution.py:48
  44.2 8.6 %all-to-all-done = f32[64,1,72]{2,1,0:T(1,128)S(1)} async-done(((f32[64,1,72]{2,1,0:T(1,128)}), f32[64,1,72]{2,1,0:T(1,128)S(1)}, u32[]{:S(2)}, u32[]{:S(2)}) %all-to-all-start) | async-done | bytes 18464 | tf_op jit(solution)/shard_map/all_to_all | solution.py:25
  52.8 0.1 reduce_sum.49
  52.9 0.0 copy-start.2
  52.9 0.6 %slice.7 = f32[1,8]{1,0:T(1,128)} slice(f32[1,72]{1,0:T(1,128)S(1)} %bitcast.31), slice={[0:1], [64:72]} | slice | bytes 64 | tf_op jit(solution)/shard_map/slice | solution.py:55
  53.4 0.0 copy-done.2
  (4 shorter events, 0.0 us)
Async XLA Ops:
  0.6 1.1 %copy-start = (bf16[1,8,64,512]{3,2,1,0:T(8,128)(2,1)S(1)}, bf16[1,8,64,512]{3,2,1,0:T(8,128)(2,1)}, u32[]{:S(2)}) copy-start(bf16[1,8,64,512]{3,2,1,0:T(8,128)(2,1)} %param.11) | copy-start | bytes 1572868
  0.6 12.2 %copy-start.1 = (bf16[1,2,64,4096]{3,2,1,0:T(8,128)(2,1)S(1)}, bf16[1,2,64,4096]{3,2,1,0:T(8,128)(2,1)}, u32[]{:S(2)}) copy-start(bf16[1,2,64,4096]{3,2,1,0:T(8,128)(2,1)} %param.10) | copy-start | bytes 3145732
  2.3 10.5 %collective-permute-start = (bf16[2,64,512]{2,1,0:T(8,128)(2,1)S(1)}, bf16[2,64,512]{2,1,0:T(8,128)(2,1)S(1)}, u32[]{:S(2)}, u32[]{:S(2)}) collective-permute-start(bf16[2,64,512]{2,1,0:T(8,128)(2,1)S(1)} %gather_fusion), channel_id=1, source_target_pairs={{0,896},{64,960},{128,0},{192,64},{256,128},{320,192},{384,256},{4... | collective-permute-start | bytes 393224 | tf_op jit(solution)/shard_map/ppermute | solution.py:41
  18.8 34.0 %all-to-all-start = ((f32[64,1,72]{2,1,0:T(1,128)}), f32[64,1,72]{2,1,0:T(1,128)S(1)}, u32[]{:S(2)}, u32[]{:S(2)}) async-start(f32[64,1,72]{2,1,0:T(1,128)} %bitcast.9), calls=%async_computation | async-start | bytes 65536 | tf_op jit(solution)/shard_map/all_to_all | solution.py:25
  52.9 0.6 %copy-start.2 = (f32[72]{0:T(128)}, f32[72]{0:T(128)S(1)}, u32[]{:S(2)}) copy-start(f32[72]{0:T(128)S(1)} %reduce_sum.49) | copy-start | bytes 868

commit v4 on v3

--- a/solution.py
+++ b/solution.py
@@ -21,9 +21,9 @@
     return (result, gain_part, bias_part)
 
 
-def reduce_over_dp(parts):
+def reduce_over_dp(parts, width):
     got = lax.all_to_all(parts, "dp", 0, 0, tiled=True)
-    return jnp.sum(got, axis=0, keepdims=True)
+    return (jnp.sum(got[:, :width], axis=0, keepdims=True), jnp.sum(got[:, width:], axis=0, keepdims=True))
 
 
 def per_device(failed, unfinished, lengths, acts, out_grads, shadow_weight, shadow_gain):
@@ -49,10 +49,10 @@
     gain_part = jnp.where(on_helper, gain_part, jnp.zeros_like(gain_part))
     bias_part = jnp.where(on_helper, bias_part, jnp.zeros_like(bias_part))
     parts = jnp.concatenate([gain_part.reshape(replicas, -1), bias_part.reshape(replicas, -1)], axis=1)
-    mine = reduce_over_dp(parts)
     gw = channels // replicas
     in_grad = collected.reshape(1, slot_count, seq_len, channels)
-    return (in_grad, mine[:, :gw], mine[:, gw:])
+    gain_share, bias_share = reduce_over_dp(parts, gw)
+    return (in_grad, gain_share, bias_share)
 
 
 def solution(mesh):

time: 53.8 us -> 54.3 us (level)
  other arithmetic: 7.82 us -> 8.88 us
  local copies, waits for them, and re-layouts: 1.66 us -> 1.07 us
    reduce_sum x1 -> x2, other arithmetic: 0.08 us -> 1.14 us  [the longest x1 0.6 us: reduce_over_dp(): jnp.sum(got[:, width:], axis=0, keepdims=True)]
    slice x1 -> x0, local copies, waits for them, and re-layouts: 0.58 us -> none  [per_device(): return (in_grad, mine[:, :gw], mine[:, gw:])]
where the time goes in v4:
time: 54.3 us; the launch traced here: 53.9 us
  starting transfers between devices  28.9 us (53%)
  other arithmetic  8.88 us (16%)
  waiting for transfers between devices  8.62 us (16%)
  matrix products  5.06 us (9%)
  between operations  1.37 us (3%)
  local copies, waits for them, and re-layouts  1.07 us (2%)
    all_to_all x1, starting transfers between devices, reduce_over_dp(): got = lax.all_to_all(parts, 'dp', 0, 0, tiled=True)  22.2 us
    all_to_all x1, waiting for transfers between devices, reduce_over_dp(): got = lax.all_to_all(parts, 'dp', 0, 0, tiled=True)  8.62 us
    ppermute x1, starting transfers between devices, per_device(): grads = lax.ppermute(chosen, 'section', pairs)  6.72 us
    dot_general x1, matrix products, local_backward(): lax.dot_general(grads, weight, (((1,), (1,)), ((), ())), preferred_elemen...  5.06 us
    select_n x1, other arithmetic, per_device(): collected = jnp.where(on_helper, collected, jnp.zeros_like(collected))  3.16 us
    reduce_sum x1, other arithmetic, local_backward(): inv_rms = lax.rsqrt(jnp.mean(wide * wide, axis=1, keepdims=True) + EPSILON)  1.52 us
  transfers between devices with their start and end apart: 2, of which 1 were waited for; matrix products, arithmetic and copies ran while one was open for 12% of the time, Pallas kernels for 0%

profile of v4, /device:TPU:1, one launch (start us, length us, event | category | flops | bytes accessed | tf_op | source)
XLA Modules:
  0.0 53.9 jit_solution(3735378611164799288)
XLA Ops:
  0.6 0.0 copy-start
  0.6 0.0 copy-start.1
  0.7 0.8 %pad_clamp_fusion = s32[1024]{0:T(1024)S(1)} fusion(s32[2]{0:T(128)} %bitcast.36), kind=kLoop, calls=%fused_computation.15 | loop fusion | flops 1024 | bytes 4104 | tf_op jit(solution)/shard_map/jit(_take)/gather | solution.py:39
  1.4 0.3 copy-done
  1.7 0.6 %gather_fusion = bf16[2,64,512]{2,1,0:T(8,128)(2,1)S(1)} fusion(bf16[8,64,512]{2,1,0:T(8,128)(2,1)S(1)} %bitcast.27, s32[1024]{0:T(1024)S(1)} %pad_clamp_fusion), kind=kCustom, calls=%fused_computation | custom fusion | bytes 262152 | tf_op jit(solution)/shard_map/jit(_take)/gather | solution.py:39
  2.3 6.7 %collective-permute-start = (bf16[2,64,512]{2,1,0:T(8,128)(2,1)S(1)}, bf16[2,64,512]{2,1,0:T(8,128)(2,1)S(1)}, u32[]{:S(2)}, u32[]{:S(2)}) collective-permute-start(bf16[2,64,512]{2,1,0:T(8,128)(2,1)S(1)} %gather_fusion), channel_id=1, source_target_pairs={{0,896},{64,960},{128,0},{192,64},{256,128},{320,192},{384,256},{4... | collective-permute-start | bytes 393224 | tf_op jit(solution)/shard_map/ppermute | solution.py:41
  9.7 0.7 %mul.57 = f32[1,4096]{1,0:T(1,128)S(1)} convert(bf16[1,4096]{1,0:T(2,128)(2,1)} %param.13) | non-fusion elementwise | flops 4096 | bytes 24576 | tf_op jit(solution)/shard_map/mul | solution.py:16
  10.4 1.5 %multiply_reduce_fusion.2 = f32[2,64]{1,0:T(2,128)S(1)} fusion(bf16[1,2,64,4096]{3,2,1,0:T(8,128)(2,1)} %param.10), kind=kLoop, calls=%fused_computation.7 | loop fusion | flops 1572736 | bytes 1049088 | tf_op jit(solution)/shard_map/reduce_sum | solution.py:11
  11.9 0.1 rsqrt.12
  12.0 0.7 %iota_compare_fusion = pred[2,64]{1,0:T(4,128)(4,1)S(1)} fusion(s32[2]{0:T(128)} %bitcast.37), kind=kLoop, calls=%fused_computation.17 | loop fusion | flops 128 | bytes 136 | tf_op jit(solution)/shard_map/lt | solution.py:43
  12.7 0.0 collective-permute-done
  12.7 0.1 convert_reduce_fusion
  12.9 0.0 copy-done.1
  12.9 5.1 %multiply_reduce_fusion = (f32[4096]{0:T(1024)S(1)}, f32[128]{0:T(128)S(1)}, f32[128,4096]{1,0:T(8,128)}) fusion(bf16[1,2,64,4096]{3,2,1,0:T(8,128)(2,1)S(1)} %copy-done.1, f32[128]{0:T(128)S(1)} %rsqrt.12, f32[4096]{0:T(1024)S(1)} %bitcast.32, bf16[128,512]{1,0:T(8,128)(2,1)S(1)} %bitcast.29, bf16[1,4096,512]{2,1,0:T(8,128)(2,1)} %param.12), kind=kOutput, calls=%fused_computation.4 | convolution fusion | flops 540536704 | bytes 7504896 | tf_op jit(solution)/shard_map/dot_general | solution.py:13
  17.9 0.1 select_n.49
  18.0 0.1 select_n.52
  18.1 0.7 %pad_maximum_fusion = f32[64,72]{1,0:T(8,128)} fusion(f32[64,8]{1,0:T(8,128)S(1)} %select_n.52, f32[64,64]{1,0:T(8,128)S(1)} %select_n.49), kind=kLoop, calls=%fused_computation.13 | loop fusion | flops 4608 | bytes 36864 | tf_op jit(solution)/shard_map/concatenate | solution.py:51
  18.8 22.2 %all-to-all-start = ((f32[64,1,72]{2,1,0:T(1,128)}), f32[64,1,72]{2,1,0:T(1,128)S(1)}, u32[]{:S(2)}, u32[]{:S(2)}) async-start(f32[64,1,72]{2,1,0:T(1,128)} %bitcast.9), calls=%async_computation | async-start | bytes 65536 | tf_op jit(solution)/shard_map/all_to_all | solution.py:25
  41.0 3.2 %fusion.2 = bf16[128,4096]{1,0:T(8,128)(2,1)} fusion(bf16[1,2,64,4096]{3,2,1,0:T(8,128)(2,1)S(1)} %copy-done.1, f32[128,4096]{1,0:T(8,128)} %get-tuple-element.7, f32[128]{0:T(128)S(1)} %broadcast_multiply_fusion, f32[4096]{0:T(1024)S(1)} %bitcast.33, f32[128]{0:T(128)S(1)} %rsqrt.12, pred[]{:T(512)S(6)} %eq.5), kind=kLoop, calls=%fused_computation.8 | loop fusion | flops 4194304 | bytes 4211713 | tf_op jit(solution)/shard_map/jit(_where)/select_n | solution.py:48
  44.2 8.6 %all-to-all-done = f32[64,1,72]{2,1,0:T(1,128)S(1)} async-done(((f32[64,1,72]{2,1,0:T(1,128)}), f32[64,1,72]{2,1,0:T(1,128)S(1)}, u32[]{:S(2)}, u32[]{:S(2)}) %all-to-all-start) | async-done | bytes 18464 | tf_op jit(solution)/shard_map/all_to_all | solution.py:25
  52.8 0.5 slice_reduce_fusion.1
  53.3 0.6 %slice_reduce_fusion = f32[8]{0:T(128)} fusion(f32[64,72]{1,0:T(8,128)S(1)} %bitcast.31), kind=kLoop, calls=%fused_computation.11 | loop fusion | flops 504 | bytes 2080 | tf_op jit(solution)/shard_map/reduce_sum | solution.py:26
  (4 shorter events, 0.0 us)
Async XLA Ops:
  0.6 1.1 %copy-start = (bf16[1,8,64,512]{3,2,1,0:T(8,128)(2,1)S(1)}, bf16[1,8,64,512]{3,2,1,0:T(8,128)(2,1)}, u32[]{:S(2)}) copy-start(bf16[1,8,64,512]{3,2,1,0:T(8,128)(2,1)} %param.11) | copy-start | bytes 1572868
  0.6 12.2 %copy-start.1 = (bf16[1,2,64,4096]{3,2,1,0:T(8,128)(2,1)S(1)}, bf16[1,2,64,4096]{3,2,1,0:T(8,128)(2,1)}, u32[]{:S(2)}) copy-start(bf16[1,2,64,4096]{3,2,1,0:T(8,128)(2,1)} %param.10) | copy-start | bytes 3145732
  2.3 10.5 %collective-permute-start = (bf16[2,64,512]{2,1,0:T(8,128)(2,1)S(1)}, bf16[2,64,512]{2,1,0:T(8,128)(2,1)S(1)}, u32[]{:S(2)}, u32[]{:S(2)}) collective-permute-start(bf16[2,64,512]{2,1,0:T(8,128)(2,1)S(1)} %gather_fusion), channel_id=1, source_target_pairs={{0,896},{64,960},{128,0},{192,64},{256,128},{320,192},{384,256},{4... | collective-permute-start | bytes 393224 | tf_op jit(solution)/shard_map/ppermute | solution.py:41
  18.8 34.0 %all-to-all-start = ((f32[64,1,72]{2,1,0:T(1,128)}), f32[64,1,72]{2,1,0:T(1,128)S(1)}, u32[]{:S(2)}, u32[]{:S(2)}) async-start(f32[64,1,72]{2,1,0:T(1,128)} %bitcast.9), calls=%async_computation | async-start | bytes 65536 | tf_op jit(solution)/shard_map/all_to_all | solution.py:25

commit v5 on v3

--- a/solution.py
+++ b/solution.py
@@ -6,19 +6,26 @@
 EPSILON = 1e-06
 
 
-def local_backward(rows, grads, weight, gain, replicas):
+def reduction_terms(rows, inv_rms, grads, weight, replicas):
     wide = rows.astype(jnp.float32)
-    inv_rms = lax.rsqrt(jnp.mean(wide * wide, axis=1, keepdims=True) + EPSILON)
+    normed = wide * inv_rms
+    grad_norm = lax.dot_general(
+        grads, weight, (((1,), (1,)), ((), ())), preferred_element_type=jnp.float32
+    )
+    gain_part = jnp.sum(grad_norm * normed, axis=0) / replicas
+    bias_part = jnp.sum(grads.astype(jnp.float32), axis=0) / replicas
+    return (gain_part, bias_part)
+
+
+def input_grad(rows, inv_rms, grads, weight, gain):
+    wide = rows.astype(jnp.float32)
     normed = wide * inv_rms
     grad_norm = lax.dot_general(
         grads, weight, (((1,), (1,)), ((), ())), preferred_element_type=jnp.float32
     )
     grad_hat = grad_norm * gain.astype(jnp.float32)[None, :]
     inner = jnp.mean(grad_hat * normed, axis=1, keepdims=True)
-    result = (inv_rms * (grad_hat - normed * inner)).astype(jnp.bfloat16)
-    gain_part = jnp.sum(grad_norm * normed, axis=0) / replicas
-    bias_part = jnp.sum(grads.astype(jnp.float32), axis=0) / replicas
-    return (result, gain_part, bias_part)
+    return (inv_rms * (grad_hat - normed * inner)).astype(jnp.bfloat16)
 
 
 def reduce_over_dp(parts):
@@ -41,15 +48,18 @@
     grads = lax.ppermute(chosen, "section", pairs)
     position = lax.broadcasted_iota(jnp.int32, grads.shape[:2], 1)
     grads = jnp.where((position < live_len[:, None])[..., None], grads, jnp.zeros_like(grads))
-    collected, gain_part, bias_part = local_backward(
-        acts[0].reshape(total_rows, channels),
-        grads.reshape(total_rows, features),
-        shadow_weight[0], shadow_gain[0], replicas)
-    collected = jnp.where(on_helper, collected, jnp.zeros_like(collected))
+    rows = acts[0].reshape(total_rows, channels)
+    grads = grads.reshape(total_rows, features)
+    wide = rows.astype(jnp.float32)
+    inv_rms = lax.rsqrt(jnp.mean(wide * wide, axis=1, keepdims=True) + EPSILON)
+    gain_part, bias_part = reduction_terms(rows, inv_rms, grads, shadow_weight[0], replicas)
     gain_part = jnp.where(on_helper, gain_part, jnp.zeros_like(gain_part))
     bias_part = jnp.where(on_helper, bias_part, jnp.zeros_like(bias_part))
     parts = jnp.concatenate([gain_part.reshape(replicas, -1), bias_part.reshape(replicas, -1)], axis=1)
+    late_rows, late_inv, late_grads, parts = lax.optimization_barrier((rows, inv_rms, grads, parts))
     mine = reduce_over_dp(parts)
+    collected = input_grad(late_rows, late_inv, late_grads, shadow_weight[0], shadow_gain[0])
+    collected = jnp.where(on_helper, collected, jnp.zeros_like(collected))
     gw = channels // replicas
     in_grad = collected.reshape(1, slot_count, seq_len, channels)
     return (in_grad, mine[:, :gw], mine[:, gw:])

time: 53.8 us -> 52.9 us (0.983)
  matrix products: 5.06 us -> 7.83 us
  waiting for transfers between devices: 8.62 us -> 6.48 us
  other arithmetic: 7.82 us -> 6.13 us
    dot_general x1 -> x2, matrix products: 5.06 us -> 7.83 us  [the longest x1 4.07 us: reduction_terms(): lax.dot_general(grads, weight, (((1,), (1,)), ((), ())), preferred_elemen...]
    all_to_all x1, waiting for transfers between devices: 8.62 us -> 6.48 us  [reduce_over_dp(): got = lax.all_to_all(parts, 'dp', 0, 0, tiled=True)]
    select_n x1, other arithmetic: 3.16 us -> 1.52 us  [per_device(): collected = jnp.where(on_helper, collected, jnp.zeros_like(collected))]
  transfers between devices with their start and end apart: 2 -> 2, of which waited for: 1 -> 1; matrix products, arithmetic and copies ran while one was open for 12% -> 16% of each run, Pallas kernels for 0% -> 0%
where the time goes in v5:
time: 52.9 us; the launch traced here: 52.6 us
  starting transfers between devices  28.9 us (55%)
  matrix products  7.83 us (15%)
  waiting for transfers between devices  6.48 us (12%)
  other arithmetic  6.13 us (12%)
  local copies, waits for them, and re-layouts  1.8 us (3%)
  between operations  1.41 us (3%)
    all_to_all x1, starting transfers between devices, reduce_over_dp(): got = lax.all_to_all(parts, 'dp', 0, 0, tiled=True)  22.2 us
    ppermute x1, starting transfers between devices, per_device(): grads = lax.ppermute(chosen, 'section', pairs)  6.72 us
    all_to_all x1, waiting for transfers between devices, reduce_over_dp(): got = lax.all_to_all(parts, 'dp', 0, 0, tiled=True)  6.48 us
    dot_general x1, matrix products, reduction_terms(): lax.dot_general(grads, weight, (((1,), (1,)), ((), ())), preferred_elemen...  4.07 us
    dot_general x1, matrix products, input_grad(): lax.dot_general(grads, weight, (((1,), (1,)), ((), ())), preferred_elemen...  3.76 us
    reduce_sum x1, other arithmetic, per_device(): inv_rms = lax.rsqrt(jnp.mean(wide * wide, axis=1, keepdims=True) + EPSILON)  1.52 us
    select_n x1, other arithmetic, per_device(): collected = jnp.where(on_helper, collected, jnp.zeros_like(collected))  1.52 us
  transfers between devices with their start and end apart: 2, of which 1 were waited for; matrix products, arithmetic and copies ran while one was open for 16% of the time, Pallas kernels for 0%

profile of v5, /device:TPU:1, one launch (start us, length us, event | category | flops | bytes accessed | tf_op | source)
XLA Modules:
  0.0 52.6 jit_solution(8520472060510490466)
XLA Ops:
  0.6 0.0 copy-start
  0.6 0.7 %pad_clamp_fusion = s32[1024]{0:T(1024)S(1)} fusion(s32[2]{0:T(128)} %bitcast.35), kind=kLoop, calls=%fused_computation.15 | loop fusion | flops 1024 | bytes 4104 | tf_op jit(solution)/shard_map/jit(_take)/gather | solution.py:46
  1.4 0.3 copy-done
  1.7 0.6 %gather_fusion = bf16[2,64,512]{2,1,0:T(8,128)(2,1)S(1)} fusion(bf16[8,64,512]{2,1,0:T(8,128)(2,1)S(1)} %bitcast.23, s32[1024]{0:T(1024)S(1)} %pad_clamp_fusion), kind=kCustom, calls=%fused_computation | custom fusion | bytes 262152 | tf_op jit(solution)/shard_map/jit(_take)/gather | solution.py:46
  2.3 6.7 %collective-permute-start = (bf16[2,64,512]{2,1,0:T(8,128)(2,1)S(1)}, bf16[2,64,512]{2,1,0:T(8,128)(2,1)S(1)}, u32[]{:S(2)}, u32[]{:S(2)}) collective-permute-start(bf16[2,64,512]{2,1,0:T(8,128)(2,1)S(1)} %gather_fusion), channel_id=1, source_target_pairs={{0,896},{64,960},{128,0},{192,64},{256,128},{320,192},{384,256},{4... | collective-permute-start | bytes 393224 | tf_op jit(solution)/shard_map/ppermute | solution.py:48
  9.7 1.5 %multiply_reduce_fusion.1 = f32[2,64]{1,0:T(2,128)S(1)} fusion(bf16[1,2,64,4096]{3,2,1,0:T(8,128)(2,1)} %param.10), kind=kLoop, calls=%fused_computation.8 | loop fusion | flops 1572736 | bytes 1049088 | tf_op jit(solution)/shard_map/reduce_sum | solution.py:54
  11.2 0.1 rsqrt.20
  11.3 0.1 rsqrt.19
  11.3 0.7 %mul.70 = f32[1,4096]{1,0:T(1,128)S(1)} convert(bf16[1,4096]{1,0:T(2,128)(2,1)} %param.13) | non-fusion elementwise | flops 4096 | bytes 24576 | tf_op jit(solution)/shard_map/mul | solution.py:26
  12.1 0.7 %iota_compare_fusion = pred[2,64]{1,0:T(4,128)(4,1)S(1)} fusion(s32[2]{0:T(128)} %bitcast.36), kind=kLoop, calls=%fused_computation.17 | loop fusion | flops 128 | bytes 136 | tf_op jit(solution)/shard_map/lt | solution.py:50
  12.8 0.0 collective-permute-done
  12.8 0.1 convert_reduce_fusion
  13.0 0.0 copy-start.1
  13.0 4.1 %fusion.2 = f32[4096]{0:T(1024)S(1)} fusion(bf16[128,4096]{1,0:T(8,128)(2,1)} %bitcast.24, bf16[128,512]{1,0:T(8,128)(2,1)S(1)} %bitcast.28, bf16[1,4096,512]{2,1,0:T(8,128)(2,1)} %param.12, f32[128]{0:T(128)S(1)} %rsqrt.20), kind=kOutput, calls=%fused_computation.9 | convolution fusion | flops 538963968 | bytes 5390848 | tf_op jit(solution)/shard_map/dot_general | solution.py:12
  17.1 0.1 select_n.48
  17.1 0.1 select_n.51
  17.2 0.7 %pad_maximum_fusion = f32[64,72]{1,0:T(8,128)} fusion(f32[64,8]{1,0:T(8,128)S(1)} %select_n.51, f32[64,64]{1,0:T(8,128)S(1)} %select_n.48), kind=kLoop, calls=%fused_computation.13 | loop fusion | flops 4608 | bytes 36864 | tf_op jit(solution)/shard_map/concatenate | solution.py:58
  17.9 22.2 %all-to-all-start = ((f32[64,1,72]{2,1,0:T(1,128)}), f32[64,1,72]{2,1,0:T(1,128)S(1)}, u32[]{:S(2)}, u32[]{:S(2)}) async-start(f32[64,1,72]{2,1,0:T(1,128)} %bitcast.10), calls=%async_computation | async-start | bytes 65536 | tf_op jit(solution)/shard_map/all_to_all | solution.py:32
  40.1 0.0 copy-done.1
  40.1 3.8 %multiply_reduce_fusion = (f32[128]{0:T(128)S(1)}, f32[128,4096]{1,0:T(8,128)S(1)}) fusion(bf16[128,4096]{1,0:T(8,128)(2,1)S(1)} %bitcast.25, f32[128]{0:T(128)S(1)} %bitcast.31, f32[4096]{0:T(1024)S(1)} %bitcast.30, bf16[128,512]{1,0:T(8,128)(2,1)S(1)} %bitcast.29, bf16[1,4096,512]{2,1,0:T(8,128)(2,1)} %param.12), kind=kOutput, calls=%fused_computation.6 | convolution fusion | flops 539492224 | bytes 7488512 | tf_op jit(solution)/shard_map/dot_general | solution.py:23
  43.9 1.5 %fusion.5 = bf16[128,4096]{1,0:T(8,128)(2,1)} fusion(f32[128,4096]{1,0:T(8,128)S(1)} %get-tuple-element.14, bf16[128,4096]{1,0:T(8,128)(2,1)S(1)} %bitcast.26, f32[128]{0:T(128)S(1)} %broadcast_multiply_fusion, f32[128]{0:T(128)S(1)} %bitcast.32, pred[]{:T(512)S(6)} %eq.5), kind=kLoop, calls=%fused_computation.10 | loop fusion | flops 3670016 | bytes 4195329 | tf_op jit(solution)/shard_map/jit(_where)/select_n | solution.py:62
  45.4 6.5 %all-to-all-done = f32[64,1,72]{2,1,0:T(1,128)S(1)} async-done(((f32[64,1,72]{2,1,0:T(1,128)}), f32[64,1,72]{2,1,0:T(1,128)S(1)}, u32[]{:S(2)}, u32[]{:S(2)}) %all-to-all-start) | async-done | bytes 18464 | tf_op jit(solution)/shard_map/all_to_all | solution.py:32
  51.9 0.1 reduce_sum.49
  52.0 0.0 copy-start.2
  52.0 0.6 %slice.7 = f32[1,8]{1,0:T(1,128)} slice(f32[1,72]{1,0:T(1,128)S(1)} %bitcast.33), slice={[0:1], [64:72]} | slice | bytes 64 | tf_op jit(solution)/shard_map/slice | solution.py:65
  52.6 0.0 copy-done.2
  (4 shorter events, 0.0 us)
Async XLA Ops:
  0.6 1.1 %copy-start = (bf16[1,8,64,512]{3,2,1,0:T(8,128)(2,1)S(1)}, bf16[1,8,64,512]{3,2,1,0:T(8,128)(2,1)}, u32[]{:S(2)}) copy-start(bf16[1,8,64,512]{3,2,1,0:T(8,128)(2,1)} %param.11) | copy-start | bytes 1572868
  2.3 10.6 %collective-permute-start = (bf16[2,64,512]{2,1,0:T(8,128)(2,1)S(1)}, bf16[2,64,512]{2,1,0:T(8,128)(2,1)S(1)}, u32[]{:S(2)}, u32[]{:S(2)}) collective-permute-start(bf16[2,64,512]{2,1,0:T(8,128)(2,1)S(1)} %gather_fusion), channel_id=1, source_target_pairs={{0,896},{64,960},{128,0},{192,64},{256,128},{320,192},{384,256},{4... | collective-permute-start | bytes 393224 | tf_op jit(solution)/shard_map/ppermute | solution.py:48
  13.0 27.2 %copy-start.1 = (bf16[1,2,64,4096]{3,2,1,0:T(8,128)(2,1)S(1)}, bf16[1,2,64,4096]{3,2,1,0:T(8,128)(2,1)}, u32[]{:S(2)}) copy-start(bf16[1,2,64,4096]{3,2,1,0:T(8,128)(2,1)} %param.10) | copy-start | bytes 3145732
  17.9 34.0 %all-to-all-start = ((f32[64,1,72]{2,1,0:T(1,128)}), f32[64,1,72]{2,1,0:T(1,128)S(1)}, u32[]{:S(2)}, u32[]{:S(2)}) async-start(f32[64,1,72]{2,1,0:T(1,128)} %bitcast.10), calls=%async_computation | async-start | bytes 65536 | tf_op jit(solution)/shard_map/all_to_all | solution.py:32
  52.0 0.6 %copy-start.2 = (f32[72]{0:T(128)}, f32[72]{0:T(128)S(1)}, u32[]{:S(2)}) copy-start(f32[72]{0:T(128)S(1)} %reduce_sum.49) | copy-start | bytes 868

commit v6 on v5

--- a/solution.py
+++ b/solution.py
@@ -51,7 +51,10 @@
     rows = acts[0].reshape(total_rows, channels)
     grads = grads.reshape(total_rows, features)
     wide = rows.astype(jnp.float32)
-    inv_rms = lax.rsqrt(jnp.mean(wide * wide, axis=1, keepdims=True) + EPSILON)
+    squares = lax.dot_general(rows, rows, (((1,), (1,)), ((), ())), preferred_element_type=jnp.float32)
+    eye = lax.broadcasted_iota(jnp.int32, squares.shape, 0) == lax.broadcasted_iota(jnp.int32, squares.shape, 1)
+    sum_sq = jnp.sum(jnp.where(eye, squares, 0.0), axis=1, keepdims=True)
+    inv_rms = lax.rsqrt(sum_sq / channels + EPSILON)
     gain_part, bias_part = reduction_terms(rows, inv_rms, grads, shadow_weight[0], replicas)
     gain_part = jnp.where(on_helper, gain_part, jnp.zeros_like(gain_part))
     bias_part = jnp.where(on_helper, bias_part, jnp.zeros_like(bias_part))

time: 52.9 us -> 52.2 us (0.987)
  other arithmetic: 6.13 us -> 3.95 us
  matrix products: 7.83 us -> 9.48 us
    dot_general x0 -> x1, matrix products: none -> 2.03 us  [per_device(): lax.dot_general(rows, rows, (((1,), (1,)), ((), ())), preferred_element_t...]
    reduce_sum x1 -> x0, other arithmetic: 1.52 us -> none  [per_device(): inv_rms = lax.rsqrt(jnp.mean(wide * wide, axis=1, keepdims=True) + EPSILON)]
    mul x1, other arithmetic: 0.74 us -> 0.02 us  [input_grad(): grad_hat = grad_norm * gain.astype(jnp.float32)[None, :]]
where the time goes in v6:
time: 52.2 us; the launch traced here: 51.8 us
  starting transfers between devices  28.9 us (55%)
  matrix products  9.48 us (18%)
  waiting for transfers between devices  6.49 us (12%)
  other arithmetic  3.95 us (8%)
  local copies, waits for them, and re-layouts  1.57 us (3%)
  between operations  1.44 us (3%)
    all_to_all x1, starting transfers between devices, reduce_over_dp(): got = lax.all_to_all(parts, 'dp', 0, 0, tiled=True)  22.2 us
    ppermute x1, starting transfers between devices, per_device(): grads = lax.ppermute(chosen, 'section', pairs)  6.72 us
    all_to_all x1, waiting for transfers between devices, reduce_over_dp(): got = lax.all_to_all(parts, 'dp', 0, 0, tiled=True)  6.48 us
    dot_general x1, matrix products, input_grad(): lax.dot_general(grads, weight, (((1,), (1,)), ((), ())), preferred_elemen...  3.76 us
    dot_general x1, matrix products, reduction_terms(): lax.dot_general(grads, weight, (((1,), (1,)), ((), ())), preferred_elemen...  3.69 us
    dot_general x1, matrix products, per_device(): lax.dot_general(rows, rows, (((1,), (1,)), ((), ())), preferred_element_t...  2.03 us
    select_n x1, other arithmetic, per_device(): collected = jnp.where(on_helper, collected, jnp.zeros_like(collected))  1.52 us
  transfers between devices with their start and end apart: 2, of which 1 were waited for; matrix products, arithmetic and copies ran while one was open for 16% of the time, Pallas kernels for 0%

profile of v6, /device:TPU:1, one launch (start us, length us, event | category | flops | bytes accessed | tf_op | source)
XLA Modules:
  0.0 51.8 jit_solution(8984321420404106034)
XLA Ops:
  0.6 0.0 copy-start
  0.6 0.0 copy-start.1
  0.7 0.0 copy-start.2
  0.7 0.8 %pad_clamp_fusion = s32[1024]{0:T(1024)S(1)} fusion(s32[2]{0:T(128)} %bitcast.40), kind=kLoop, calls=%fused_computation.17 | loop fusion | flops 1024 | bytes 4104 | tf_op jit(solution)/shard_map/jit(_take)/gather | solution.py:46
  1.4 0.3 copy-done
  1.7 0.6 %gather_fusion = bf16[2,64,512]{2,1,0:T(8,128)(2,1)S(1)} fusion(bf16[8,64,512]{2,1,0:T(8,128)(2,1)S(1)} %bitcast.27, s32[1024]{0:T(1024)S(1)} %pad_clamp_fusion), kind=kCustom, calls=%fused_computation | custom fusion | bytes 262152 | tf_op jit(solution)/shard_map/jit(_take)/gather | solution.py:46
  2.3 6.7 %collective-permute-start = (bf16[2,64,512]{2,1,0:T(8,128)(2,1)S(1)}, bf16[2,64,512]{2,1,0:T(8,128)(2,1)S(1)}, u32[]{:S(2)}, u32[]{:S(2)}) collective-permute-start(bf16[2,64,512]{2,1,0:T(8,128)(2,1)S(1)} %gather_fusion), channel_id=1, source_target_pairs={{0,896},{64,960},{128,0},{192,64},{256,128},{320,192},{384,256},{4... | collective-permute-start | bytes 393224 | tf_op jit(solution)/shard_map/ppermute | solution.py:48
  9.7 0.7 %iota_compare_fusion.1 = pred[2,64]{1,0:T(4,128)(4,1)S(1)} fusion(s32[2]{0:T(128)} %bitcast.41), kind=kLoop, calls=%fused_computation.19 | loop fusion | flops 128 | bytes 136 | tf_op jit(solution)/shard_map/lt | solution.py:50
  10.4 2.0 %fusion.5 = f32[128]{0:T(128)S(1)} fusion(bf16[128,4096]{1,0:T(8,128)(2,1)} %bitcast.28), kind=kOutput, calls=%fused_computation.10 | convolution fusion | flops 134266752 | bytes 1049088 | tf_op jit(solution)/shard_map/dot_general | solution.py:54
  12.4 0.0 copy-done.2
  12.5 0.0 collective-permute-done
  12.5 0.1 convert_reduce_fusion
  12.6 0.0 copy-done.1
  12.6 3.7 %fusion.2 = f32[4096]{0:T(1024)S(1)} fusion(bf16[128,4096]{1,0:T(8,128)(2,1)S(1)} %bitcast.29, bf16[128,512]{1,0:T(8,128)(2,1)S(1)} %bitcast.33, bf16[1,4096,512]{2,1,0:T(8,128)(2,1)} %param.12, f32[128]{0:T(128)S(1)} %get-tuple-element.13), kind=kOutput, calls=%fused_computation.8 | convolution fusion | flops 538963968 | bytes 5390848 | tf_op jit(solution)/shard_map/dot_general | solution.py:12
  16.3 0.1 select_n.53
  16.4 0.1 select_n.56
  16.5 0.7 %pad_maximum_fusion = f32[64,72]{1,0:T(8,128)} fusion(f32[64,8]{1,0:T(8,128)S(1)} %select_n.56, f32[64,64]{1,0:T(8,128)S(1)} %select_n.53), kind=kLoop, calls=%fused_computation.15 | loop fusion | flops 4608 | bytes 36864 | tf_op jit(solution)/shard_map/concatenate | solution.py:61
  17.2 22.2 %all-to-all-start = ((f32[64,1,72]{2,1,0:T(1,128)}), f32[64,1,72]{2,1,0:T(1,128)S(1)}, u32[]{:S(2)}, u32[]{:S(2)}) async-start(f32[64,1,72]{2,1,0:T(1,128)} %bitcast.11), calls=%async_computation | async-start | bytes 65536 | tf_op jit(solution)/shard_map/all_to_all | solution.py:32
  39.4 3.8 %multiply_reduce_fusion = (f32[128]{0:T(128)S(1)}, f32[128,4096]{1,0:T(8,128)S(1)}) fusion(bf16[128,4096]{1,0:T(8,128)(2,1)S(1)} %bitcast.30, f32[128]{0:T(128)S(1)} %bitcast.36, f32[4096]{0:T(1024)S(1)} %bitcast.35, bf16[128,512]{1,0:T(8,128)(2,1)S(1)} %bitcast.34, bf16[1,4096,512]{2,1,0:T(8,128)(2,1)} %param.12), kind=kOutput, calls=%fused_computation.6 | convolution fusion | flops 539492224 | bytes 7488512 | tf_op jit(solution)/shard_map/dot_general | solution.py:23
  43.2 1.5 %fusion.6 = bf16[128,4096]{1,0:T(8,128)(2,1)} fusion(f32[128,4096]{1,0:T(8,128)S(1)} %get-tuple-element.16, bf16[128,4096]{1,0:T(8,128)(2,1)S(1)} %bitcast.31, f32[128]{0:T(128)S(1)} %broadcast_multiply_fusion, f32[128]{0:T(128)S(1)} %bitcast.37, pred[]{:T(512)S(6)} %eq.8), kind=kLoop, calls=%fused_computation.11 | loop fusion | flops 3670016 | bytes 4195329 | tf_op jit(solution)/shard_map/jit(_where)/select_n | solution.py:65
  44.7 6.5 %all-to-all-done = f32[64,1,72]{2,1,0:T(1,128)S(1)} async-done(((f32[64,1,72]{2,1,0:T(1,128)}), f32[64,1,72]{2,1,0:T(1,128)S(1)}, u32[]{:S(2)}, u32[]{:S(2)}) %all-to-all-start) | async-done | bytes 18464 | tf_op jit(solution)/shard_map/all_to_all | solution.py:32
  51.2 0.1 reduce_sum.49
  51.2 0.0 copy-start.3
  51.2 0.6 %slice.7 = f32[1,8]{1,0:T(1,128)} slice(f32[1,72]{1,0:T(1,128)S(1)} %bitcast.38), slice={[0:1], [64:72]} | slice | bytes 64 | tf_op jit(solution)/shard_map/slice | solution.py:68
  51.8 0.0 copy-done.3
  (5 shorter events, 0.0 us)
Async XLA Ops:
  0.6 1.1 %copy-start = (bf16[1,8,64,512]{3,2,1,0:T(8,128)(2,1)S(1)}, bf16[1,8,64,512]{3,2,1,0:T(8,128)(2,1)}, u32[]{:S(2)}) copy-start(bf16[1,8,64,512]{3,2,1,0:T(8,128)(2,1)} %param.11) | copy-start | bytes 1572868
  0.6 12.0 %copy-start.1 = (bf16[1,2,64,4096]{3,2,1,0:T(8,128)(2,1)S(1)}, bf16[1,2,64,4096]{3,2,1,0:T(8,128)(2,1)}, u32[]{:S(2)}) copy-start(bf16[1,2,64,4096]{3,2,1,0:T(8,128)(2,1)} %param.10) | copy-start | bytes 3145732
  0.7 11.8 %copy-start.2 = (bf16[1,4096]{1,0:T(2,128)(2,1)S(1)}, bf16[1,4096]{1,0:T(2,128)(2,1)}, u32[]{:S(2)}) copy-start(bf16[1,4096]{1,0:T(2,128)(2,1)} %param.13) | copy-start | bytes 24580
  2.3 10.2 %collective-permute-start = (bf16[2,64,512]{2,1,0:T(8,128)(2,1)S(1)}, bf16[2,64,512]{2,1,0:T(8,128)(2,1)S(1)}, u32[]{:S(2)}, u32[]{:S(2)}) collective-permute-start(bf16[2,64,512]{2,1,0:T(8,128)(2,1)S(1)} %gather_fusion), channel_id=1, source_target_pairs={{0,896},{64,960},{128,0},{192,64},{256,128},{320,192},{384,256},{4... | collective-permute-start | bytes 393224 | tf_op jit(solution)/shard_map/ppermute | solution.py:48
  17.2 34.0 %all-to-all-start = ((f32[64,1,72]{2,1,0:T(1,128)}), f32[64,1,72]{2,1,0:T(1,128)S(1)}, u32[]{:S(2)}, u32[]{:S(2)}) async-start(f32[64,1,72]{2,1,0:T(1,128)} %bitcast.11), calls=%async_computation | async-start | bytes 65536 | tf_op jit(solution)/shard_map/all_to_all | solution.py:32
  51.2 0.6 %copy-start.3 = (f32[72]{0:T(128)}, f32[72]{0:T(128)S(1)}, u32[]{:S(2)}) copy-start(f32[72]{0:T(128)S(1)} %reduce_sum.49) | copy-start | bytes 868
